TPU v7x, 512 devices: a whole 4x4x16 slice. The times are simulated.
512 devices in a mesh: dp: 32 (over z, core), seq: 16 (over y, x).
Axes of the slice: x: 4, y: 4, z: 16, core: 2. Of those that a mesh axis runs over, the one named last changes fastest.
Arguments:
- mixer_in: bfloat16 [131072, 2816], P(('dp', 'seq')), parts along dimension 0, may hold values from -92 to 92
- gate_input: bfloat16 [131072, 2560], P(('dp', 'seq')), parts along dimension 0, may hold values from -6 to 6
- step_raw: bfloat16 [131072, 40], P(('dp', 'seq')), parts along dimension 0, may hold values from -6 to 6
- lengths: int32 [96], P('dp'), parts along dimension 0, may hold values from 1 to 2048, 4096 in all
- deal_order: int32 [512], P('dp'), parts along dimension 0, may hold values from 0 to 15, as said below
- conv_weight: float32 [4, 2816], replicated, may hold values from -3 to 3
- conv_bias: float32 [2816], replicated, may hold values from -3 to 3
- step_bias: float32 [40], replicated, may hold values from -4 to -1
- decay_rate: float32 [40], replicated, may hold values from 0.01 to 2
- skip_gain: float32 [40], replicated, may hold values from 0.5 to 1.5
- norm_gain: float32 [2560], replicated, may hold values from 0.5 to 1.5
Outputs:
- mixed_out: bfloat16 [131072, 2560], P(('dp', 'seq')), parts along dimension 0
- final_states: float32 [96, 2560, 128], P('dp', 'seq'), parts along dimension 0
There are 32 independent parts, one for each index of `dp`. A program takes and returns all parts, laid end to end along the dimension named above; an argument that names none is the same for every part. Nothing has to cross between parts.
Inputs may be any that keep to these rules, and one draw needn't show every extreme that they name: The prompt lengths sum to 4096 and the longest is exactly 2048. `deal_order`: every sequence stretch stands in exactly one dealt slot.
All inputs are finite; a program needn't handle non-finite values.
Results may differ from a plain program's by a relative error of at most 0.005.
Values may be sent and summed in bfloat16 or wider, within the bound.
No kernel may reach another device: no remote copies, remote signals or barrier semaphores. Data moves between devices by JAX's collectives and lax.ppermute only.
A program may use at most 128 MiB of HBM per device.

v0:
```python
import jax
import jax.numpy as jnp
from jax import lax
from jax.sharding import PartitionSpec as P

HEADS = 40
HEAD_DIM = 64
STATE = 128
KERNEL = 4
STRETCH = 256
DOCS = 3
INNER = 2560
CHANNELS = 2816


def doc_index(ends, positions):
    return jnp.sum((ends[None, :] <= positions[:, None]).astype(jnp.int32), axis=1)


def body(
    mixer_in,
    gate_input,
    step_raw,
    lengths,
    deal_order,
    conv_weight,
    conv_bias,
    step_bias,
    decay_rate,
    skip_gain,
    norm_gain,
):
    myself = lax.axis_index("seq")
    local_rows = mixer_in.shape[0]
    stretches_here = local_rows // STRETCH
    stretch_total = deal_order.shape[0]
    ends = jnp.cumsum(lengths)
    all_stretches = jnp.arange(stretch_total, dtype=jnp.int32)
    my_stretches = lax.dynamic_slice_in_dim(deal_order, myself * stretches_here, stretches_here)
    lane = jnp.arange(STRETCH, dtype=jnp.int32)
    own_doc = doc_index(
        ends, (my_stretches[:, None] * STRETCH + lane[None, :]).reshape(-1)
    ).reshape(stretches_here, STRETCH)
    prev_own = jnp.where(my_stretches > 0, doc_index(ends, my_stretches * STRETCH - 1), -1)
    blocks_in = mixer_in.reshape(stretches_here, STRETCH, CHANNELS)
    tails = blocks_in[:, STRETCH - (KERNEL - 1) :, :]
    step_blocks = step_raw.reshape(stretches_here, STRETCH, HEADS)
    step = jax.nn.softplus(step_blocks.astype(jnp.float32) + step_bias)
    log_decay = -decay_rate * step
    all_tails, all_steps = (
        lax.all_gather(tails, "seq", axis=0, tiled=True),
        lax.all_gather(step_blocks, "seq", axis=0, tiled=True),
    )
    totals = jnp.sum(
        -decay_rate * jax.nn.softplus(all_steps.astype(jnp.float32) + step_bias), axis=1
    )
    slot_map = (deal_order[:, None] == all_stretches[None, :]).astype(jnp.float32)
    packed_totals = jnp.dot(slot_map.T, totals, precision=lax.Precision.HIGHEST)
    prefix = jnp.cumsum(packed_totals, axis=0)
    base = jnp.concatenate([jnp.zeros((1, HEADS), jnp.float32), prefix[:-1]], 0)
    pick_own = (my_stretches[:, None] == all_stretches[None, :]).astype(jnp.float32)
    base_own = jnp.dot(pick_own, base, precision=lax.Precision.HIGHEST)
    running = base_own[:, None, :] + jnp.cumsum(log_decay, axis=1)
    prev_pick = (deal_order[None, :] == my_stretches[:, None] - 1).astype(jnp.bfloat16)
    prev_rows = jnp.einsum(
        "is,skc->ikc", prev_pick, all_tails, preferred_element_type=jnp.float32
    ).astype(jnp.bfloat16)
    extended = jnp.concatenate([prev_rows, blocks_in], 1)
    lead = (
        my_stretches[:, None] * STRETCH
        - (KERNEL - 1)
        + jnp.arange(KERNEL - 1, dtype=jnp.int32)[None, :]
    ).reshape(-1)
    ext_doc = jnp.concatenate(
        [doc_index(ends, lead).reshape(stretches_here, KERNEL - 1), own_doc], 1
    )
    accum = jnp.zeros((stretches_here, STRETCH, CHANNELS), jnp.float32) + conv_bias
    for offset in range(KERNEL):
        keep = (ext_doc[:, offset : offset + STRETCH] == own_doc).astype(jnp.float32)
        accum = (
            accum
            + conv_weight[offset]
            * extended[:, offset : offset + STRETCH, :].astype(jnp.float32)
            * keep[..., None]
        )
    mixed = jax.nn.silu(accum).astype(jnp.bfloat16)
    values = mixed[..., :INNER]
    input_map = mixed[..., INNER : INNER + STATE]
    output_map = mixed[..., INNER + STATE :]
    scaled = (values.astype(jnp.float32) * jnp.repeat(step, HEAD_DIM, axis=2)).astype(jnp.bfloat16)
    end_weight = jnp.exp(
        jnp.where((own_doc == own_doc[:, -1:])[..., None], running[:, -1:, :] - running, -jnp.inf)
    )
    weighted = (scaled.astype(jnp.float32) * jnp.repeat(end_weight, HEAD_DIM, axis=2)).astype(
        jnp.bfloat16
    )
    states = jnp.einsum("isk,isn->ikn", weighted, input_map, preferred_element_type=jnp.float32)
    source_pick = (deal_order[:, None] == all_stretches[None, :]).astype(jnp.float32)
    source_end = jnp.dot(source_pick, prefix, precision=lax.Precision.HIGHEST)
    source_doc = doc_index(ends, deal_order * STRETCH + STRETCH - 1)
    allowed = (deal_order[None, :] < my_stretches[:, None]) & (
        source_doc[None, :] == prev_own[:, None]
    )
    spans = jnp.exp(
        jnp.where(allowed[..., None], base_own[:, None, :] - source_end[None, :, :], -jnp.inf)
    )
    state_in = jnp.einsum(
        "ick,ckn->ikn",
        jnp.repeat(spans, HEAD_DIM, axis=2),
        lax.all_gather(states, "seq", axis=0, tiled=True),
        precision=lax.Precision.HIGHEST,
    )
    later = lane[:, None] >= lane[None, :]
    direct_gain = jnp.repeat(skip_gain, HEAD_DIM)[None, :]

    def stretch_out(inputs):
        values_c, scaled_c, keys_c, queries_c, running_c, doc_c, base_c, prev_c, state_c = inputs
        scores = jnp.dot(queries_c, keys_c.T, preferred_element_type=jnp.float32)
        same = (doc_c[:, None] == doc_c[None, :]) & later
        spans = running_c.T[:, :, None] - running_c.T[:, None, :]
        mixing = (scores[None] * jnp.exp(jnp.where(same[None], spans, -jnp.inf))).astype(
            jnp.bfloat16
        )
        within = jnp.einsum(
            "hts,shp->thp",
            mixing,
            scaled_c.reshape(STRETCH, HEADS, HEAD_DIM),
            preferred_element_type=jnp.float32,
        ).reshape(STRETCH, INNER)
        readout = jnp.dot(
            queries_c, state_c.astype(jnp.bfloat16).T, preferred_element_type=jnp.float32
        )
        carry_weight = jnp.exp(
            jnp.where((doc_c == prev_c)[:, None], running_c - base_c[None, :], -jnp.inf)
        )
        return (
            within
            + readout * jnp.repeat(carry_weight, HEAD_DIM, axis=1)
            + values_c.astype(jnp.float32) * direct_gain
        )

    outputs = lax.map(
        stretch_out,
        (values, scaled, input_map, output_map, running, own_doc, base_own, prev_own, state_in),
    )
    gated = outputs.reshape(local_rows, INNER) * jax.nn.silu(gate_input.astype(jnp.float32))
    normed = gated * lax.rsqrt(jnp.mean(gated * gated, axis=1, keepdims=True) + 1e-05) * norm_gain
    mixed_out = normed.astype(jnp.bfloat16)
    slot_numbers = jnp.arange(stretches_here, dtype=jnp.int32)

    def one_doc(document):
        last = lax.dynamic_index_in_dim(ends, document, keepdims=False) - 1
        owner = last // STRETCH
        match = my_stretches == owner
        slot = jnp.sum(jnp.where(match, slot_numbers, 0))

        def present():
            within_pos = last - owner * STRETCH
            running_c = lax.dynamic_index_in_dim(running, slot, keepdims=False)
            running_e = lax.dynamic_index_in_dim(running_c, within_pos, keepdims=False)
            doc_c = lax.dynamic_index_in_dim(own_doc, slot, keepdims=False)
            scaled_c = lax.dynamic_index_in_dim(scaled, slot, keepdims=False)
            keys_c = lax.dynamic_index_in_dim(input_map, slot, keepdims=False)
            base_c = lax.dynamic_index_in_dim(base_own, slot, keepdims=False)
            prev_c = lax.dynamic_index_in_dim(prev_own, slot, keepdims=False)
            state_c = lax.dynamic_index_in_dim(state_in, slot, keepdims=False)
            weight = jnp.exp(
                jnp.where((doc_c == document)[:, None], running_e[None, :] - running_c, -jnp.inf)
            )
            final_weighted = (
                scaled_c.astype(jnp.float32) * jnp.repeat(weight, HEAD_DIM, axis=1)
            ).astype(jnp.bfloat16)
            part = jnp.dot(final_weighted.T, keys_c, preferred_element_type=jnp.float32)
            carry_weight = jnp.exp(jnp.where(prev_c == document, running_e - base_c, -jnp.inf))
            return part + jnp.repeat(carry_weight, HEAD_DIM)[:, None] * state_c

        def absent():
            return jnp.zeros((INNER, STATE), jnp.float32)

        return lax.cond(jnp.any(match), present, absent)

    every_doc = jnp.transpose(lax.map(one_doc, jnp.arange(DOCS, dtype=jnp.int32)), (1, 0, 2))
    kept = lax.psum_scatter(
        every_doc.astype(jnp.bfloat16), "seq", scatter_dimension=0, tiled=True
    ).astype(jnp.float32)
    final_states = jnp.transpose(kept, (1, 0, 2))
    return (mixed_out, final_states)


def solution(mesh):
    return jax.shard_map(
        body,
        mesh=mesh,
        in_specs=(
            P(("dp", "seq"), None),
            P(("dp", "seq"), None),
            P(("dp", "seq"), None),
            P("dp"),
            P("dp"),
            P(),
            P(),
            P(),
            P(),
            P(),
            P(),
        ),
        out_specs=(P(("dp", "seq"), None), P("dp", "seq", None)),
        check_vma=False,
    )
```

profile of v0, /device:TPU:2, one launch (start us, length us, event | category | flops | bytes accessed | tf_op | source)
XLA Modules:
  0.0 391.7 jit_solution(15185379277083827339)
XLA Ops:
  7.9 26.9 %all-gather = bf16[4096,40]{0,1:T(8,128)(2,1)S(1)} all-gather(bf16[256,40]{0,1:T(8,128)(2,1)} %param.17), channel_id=2, replica_groups=mesh['dp'=32,'seq'=16] {'seq'}, dimensions={0}, use_global_device_ids=true | all-gather | bytes 348160 | tf_op jit(solution)/shard_map/all_gather | solution.py:52
  36.5 1.2 dynamic_slice.62
  41.6 21.6 %all_gather.9 = bf16[16,3,2816]{2,1,0:T(4,128)(2,1)S(1)} all-gather(bf16[1,3,2816]{2,1,0:T(4,128)(2,1)S(1)} %slice.76), channel_id=1, replica_groups=mesh['dp'=32,'seq'=16] {'seq'}, dimensions={0}, use_global_device_ids=true | all-gather | bytes 287232 | tf_op jit(solution)/shard_map/all_gather | solution.py:51
  64.1 1.1 slice_reduce_fusion.5
  65.4 2.1 copy.73
  73.3 2.1 copy.78
  75.5 5.9 %multiply_convert_fusion.2 = bf16[1,256,2816]{2,1,0:T(8,128)(2,1)S(1)} fusion(bf16[256,2816]{1,0:T(8,128)(2,1)} %param.15, bf16[1,3,2816]{2,1,0:T(4,128)(2,1)S(1)} %copy.108, bf16[1,256,2816]{2,1,0:T(8,128)(2,1)} %bitcast.153, f32[2816]{0:T(1024)S(1)} %get-tuple-element.357, f32[256]{0:T(256)S(1)} %bitcast.173, f32[2816]{0:T(1024)S(1)} %get-tuple-element.358, ...), kind=kLoop, calls=%fused_computation.33 | loop fusion | flops 20905984 | bytes 4401664 | tf_op jit(solution)/shard_map/convert_element_type | solution.py:86
  81.8 1.9 copy-done.1
  83.7 1.8 fusion.25
  85.8 1.4 copy.74
  88.2 146.0 %all-gather.4.cloned.1.call-done = f32[40960,128]{1,0:T(8,128)} async-done(((f32[2560,128]{1,0:T(8,128)}), f32[40960,128]{1,0:T(8,128)}) %all-gather.4.cloned.1.call-update) | async-done | bytes 20971536 | tf_op jit(solution)/shard_map/all_gather | solution.py:110
  234.4 38.9 %fusion.6 = f32[2560,1,128]{2,1,0:T(1,128)S(1)} fusion(f32[16,2560,1]{0,2,1:T(1,128)S(1)} %bitcast.151, f32[16,2560,128]{2,1,0:T(8,128)} %bitcast.147), kind=kOutput, calls=%fused_computation.15 | convolution fusion | flops 62914560 | bytes 22446080 | tf_op jit(solution)/shard_map/ick,ckn->ikn/dot_general | solution.py:107
  273.3 20.2 %while.17 = (s32[]{:T(128)}, bf16[3,2560,128]{2,1,0:T(8,128)(2,1)}, s32[3]{0:T(128)S(1)}, s32[3]{0:T(128)S(1)}, s32[1]{0:T(128)}, /*index=5*/bf16[1,256,2560]{1,...) while((s32[]{:T(128)}, bf16[3,2560,128]{2,1,0:T(8,128)(2,1)}, ...), condition=%wide.region_13.14_spmd, body=%wide.region_10.13_spmd.sunk | while | flops 170742112 | bytes 7442075 | solution.py:182
  277.7 4.0 %conditional.2 = (bf16[1,2560,128]{2,1,0:T(8,128)(2,1)S(1)}) conditional(s32[]{:T(128)} %bitcast.143, () %tuple.66, (bf16[1,256,2560]{1,2,0:T(8,128)(2,1)}, s32[]{:T(128)}, s32[1,256]{1,0:T(1,128)S(1)}, s32[]{:T(128)}, s32[]{:T(128)}, /*index=5*/f32[1,256,40]{1,2,0:T(8,128)S(1)}, bf16[1,256,128]{2,1,0:T(8,128)(2,1)S(1)}, s32[1]{0:T(128)}, ...), branch_computations={%region_11.11_spmd, %region_12.12_spmd} | conditional | flops 170742096 | bytes 6130356 | solution.py:180
  278.6 1.7 fusion.1
  293.5 1.1 fusion.36
  294.6 5.1 %fusion.8 = f32[40,64,256]{2,1,0:T(8,128)} fusion(bf16[256,40,64]{0,2,1:T(8,128)(2,1)} %bitcast.28, f32[40,256]{1,0:T(8,128)S(1)} %bitcast.154, f32[256,256]{1,0:T(8,128)S(1)} %fusion.36, pred[256,256]{1,0:T(8,128)(4,1)S(1)} %fusion.34), kind=kOutput, calls=%fused_computation.18 | convolution fusion | flops 346030080 | bytes 4300800 | tf_op jit(solution)/shard_map/while/body/eval_jaxpr/hts,shp->thp/dot_general | solution.py:124
  299.7 3.2 copy.80
  303.0 1.7 broadcast_in_dim.192
  304.7 3.4 copy.79
  308.2 4.6 %multiply_reduce_fusion = (f32[256]{0:T(256)S(1)}, f32[256,2560]{1,0:T(8,128)S(1)}) fusion(bf16[256,2560]{1,0:T(8,128)(2,1)S(1)} %copy-done.8, f32[2560]{0:T(1024)S(1)} %mul.239, bf16[1,256,2816]{2,1,0:T(8,128)(2,1)} %copy-done.2, f32[256,2560]{1,0:T(8,128)} %copy.80, f32[256,2560]{1,0:T(8,128)} %copy.79, f32[2560,128]{1,0:T(8,128)S(1)} %bitcast.146), kind=kOutput, calls=%fused_computation.40 | convolution fusion | flops 176619264 | bytes 11873280 | tf_op jit(solution)/shard_map/while/body/eval_jaxpr/dot_general | solution.py:130
  312.9 1.3 multiply_convert_fusion.3
  314.2 69.0 %reduce-scatter.2.cloned.1.call-done = bf16[160,3,128]{2,0,1:T(8,128)(2,1)} async-done(((bf16[2560,3,128]{2,0,1:T(8,128)(2,1)}), bf16[160,3,128]{2,0,1:T(8,128)(2,1)}) %reduce-scatter.2.cloned.1.call-update) | async-done | bytes 122896 | tf_op jit(solution)/shard_map/reduce_scatter | solution.py:183
  383.3 1.6 convert_bitcast_fusion.2
  (91 shorter events, 20.9 us)
Async XLA Ops:
  7.2 227.1 %all-gather.4.cloned.1.call-start = ((), (), s32[]{:S(2)}) async-start(), calls=%async_computation.2 | async-start | bytes 22282240 | tf_op jit(solution)/shard_map/all_gather | solution.py:110
  65.4 3.7 copy-start.6
  67.5 2.1 copy-start.5
  73.3 2.1 copy-start.4
  75.5 5.9 %copy-start = (f32[1,256,2560]{2,1,0:T(8,128)S(1)}, f32[1,256,2560]{2,1,0:T(8,128)}, u32[]{:S(2)}) copy-start(f32[1,256,2560]{2,1,0:T(8,128)} %copy.73) | copy-start | bytes 7864324
  81.4 153.0 %copy-start.2 = (bf16[1,256,2816]{2,1,0:T(8,128)(2,1)}, bf16[1,256,2816]{2,1,0:T(8,128)(2,1)S(1)}, u32[]{:S(2)}) copy-start(bf16[1,256,2816]{2,1,0:T(8,128)(2,1)S(1)} %multiply_convert_fusion.2) | copy-start | bytes 4325380
  81.4 2.3 copy-start.1
  85.5 297.7 %reduce-scatter.2.cloned.1.call-start = ((), (), s32[]{:S(2)}) async-start(), calls=%async_computation.1 | async-start | bytes 2088960 | tf_op jit(solution)/shard_map/reduce_scatter | solution.py:183
  304.7 3.4 copy-start.7
  304.7 3.5 copy-start.8
  308.2 4.7 %copy-start.3 = (f32[2560]{0:T(1024)S(1)}, f32[2560]{0:T(1024)}, u32[]{:S(2)}) copy-start(f32[2560]{0:T(1024)} %param.25) | copy-start | bytes 30724
Sparse Core Ops, SparseCore 0:
  85.7 148.5 all-gather.3
  293.6 89.6 reduce-scatter.1
where the time goes:
time: 393 us; the launch traced here: 392 us
  waiting for transfers between devices  215 us (55%)
  matrix products  54 us (14%)
  blocking collectives  48.5 us (12%)
  local copies, waits for them, and re-layouts  28.5 us (7%)
  other arithmetic  18 us (5%)
  between operations  17 us (4%)
  loops' own time  10.3 us (3%)
    all_gather x1, waiting for transfers between devices, body(): lax.all_gather(states, 'seq', axis=0, tiled=True)  146 us
    reduce_scatter x1, waiting for transfers between devices, body(): lax.psum_scatter(every_doc.astype(jnp.bfloat16), 'seq', scatter_dimension...  69 us
    dot_general x1, matrix products, body(): jnp.einsum('ick,ckn->ikn', jnp.repeat(spans, HEAD_DIM, axis=2), lax.all_g...  38.9 us
    all_gather x1, blocking collectives, body(): lax.all_gather(step_blocks, 'seq', axis=0, tiled=True)  26.9 us
    all_gather x1, blocking collectives, body(): lax.all_gather(tails, 'seq', axis=0, tiled=True)  21.6 us
    another operation x1, loops' own time, body(): lax.map(one_doc, jnp.arange(DOCS, dtype=jnp.int32))  9.57 us
  transfers between devices with their start and end apart: 2, of which 2 were waited for; matrix products, arithmetic and copies ran while one was open for 6% of the time, Pallas kernels for 0%

commit v1 on v0

--- a/solution.py
+++ b/solution.py
@@ -1,3 +1,4 @@
+import functools
 import jax
 import jax.numpy as jnp
 from jax import lax
@@ -11,6 +12,17 @@
 DOCS = 3
 INNER = 2560
 CHANNELS = 2816
+
+
+def lead_body(mat, dim_no):
+    s_next = jax.lax.axis_size("seq")
+    item_now = jnp.stack([mat] * s_next)
+    field_out = jax.lax.all_to_all(item_now, axis_name="seq", split_axis=0, concat_axis=0)
+    tile_out = jnp.concatenate(field_out, dim_no)
+    return tile_out
+
+
+refer_the_patch = functools.partial(lead_body, dim_no=0)
 
 
 def doc_index(ends, positions):
@@ -48,7 +60,7 @@
     step = jax.nn.softplus(step_blocks.astype(jnp.float32) + step_bias)
     log_decay = -decay_rate * step
     all_tails, all_steps = (
-        lax.all_gather(tails, "seq", axis=0, tiled=True),
+        refer_the_patch(tails),
         lax.all_gather(step_blocks, "seq", axis=0, tiled=True),
     )
     totals = jnp.sum(

time: 393 us -> 378 us (0.962)
  blocking collectives: 48.5 us -> 23.8 us
  starting transfers between devices: 0.26 us -> 9.48 us
    all_gather x1 -> x0, blocking collectives: 21.6 us -> none  [body(): lax.all_gather(tails, 'seq', axis=0, tiled=True)]
    all_to_all x0 -> x1, starting transfers between devices: none -> 9.22 us  [lead_body(): jax.lax.all_to_all(item_now, axis_name='seq', split_axis=0, concat_axis=0)]
  transfers between devices with their start and end apart: 2 -> 3, of which waited for: 2 -> 2; matrix products, arithmetic and copies ran while one was open for 6% -> 10% of each run, Pallas kernels for 0% -> 0%
where the time goes in v1:
time: 378 us; the launch traced here: 377 us
  waiting for transfers between devices  215 us (57%)
  matrix products  53.4 us (14%)
  local copies, waits for them, and re-layouts  27.8 us (7%)
  blocking collectives  23.8 us (6%)
  other arithmetic  20.3 us (5%)
  between operations  17 us (4%)
  loops' own time  10.3 us (3%)
  starting transfers between devices  9.48 us (3%)
    all_gather x1, waiting for transfers between devices, body(): lax.all_gather(states, 'seq', axis=0, tiled=True)  146 us
    reduce_scatter x1, waiting for transfers between devices, body(): lax.psum_scatter(every_doc.astype(jnp.bfloat16), 'seq', scatter_dimension...  69 us
    dot_general x1, matrix products, body(): jnp.einsum('ick,ckn->ikn', jnp.repeat(spans, HEAD_DIM, axis=2), lax.all_g...  38.9 us
    all_gather x1, blocking collectives, body(): lax.all_gather(step_blocks, 'seq', axis=0, tiled=True)  23.8 us
    another operation x1, loops' own time, body(): lax.map(one_doc, jnp.arange(DOCS, dtype=jnp.int32))  9.58 us
    all_to_all x1, starting transfers between devices, lead_body(): jax.lax.all_to_all(item_now, axis_name='seq', split_axis=0, concat_axis=0)  9.22 us
  transfers between devices with their start and end apart: 3, of which 2 were waited for; matrix products, arithmetic and copies ran while one was open for 10% of the time, Pallas kernels for 0%

profile of v1, /device:TPU:2, one launch (start us, length us, event | category | flops | bytes accessed | tf_op | source)
XLA Modules:
  0.0 377.2 jit_solution(908125450925536559)
XLA Ops:
  8.8 9.2 %all-to-all-start = ((bf16[16,1,3,2816]{3,2,1,0:T(4,128)(2,1)}), bf16[16,1,3,2816]{3,2,1,0:T(4,128)(2,1)S(1)}, u32[]{:S(2)}, u32[]{:S(2)}) async-start(bf16[16,1,3,2816]{3,2,1,0:T(4,128)(2,1)} %stack.2), calls=%async_computation | async-start | bytes 720896 | tf_op jit(solution)/shard_map/all_to_all | solution.py:20
  18.8 23.8 %all-gather = bf16[4096,40]{0,1:T(8,128)(2,1)S(1)} all-gather(bf16[256,40]{0,1:T(8,128)(2,1)} %param.17), channel_id=2, replica_groups=mesh['dp'=32,'seq'=16] {'seq'}, dimensions={0}, use_global_device_ids=true | all-gather | bytes 348160 | tf_op jit(solution)/shard_map/all_gather | solution.py:64
  44.2 1.2 dynamic_slice.62
  47.0 1.1 slice_reduce_fusion.5
  55.4 2.1 copy.73
  57.8 2.1 copy.78
  60.2 5.9 %multiply_convert_fusion.2 = bf16[1,256,2816]{2,1,0:T(8,128)(2,1)S(1)} fusion(bf16[256,2816]{1,0:T(8,128)(2,1)} %param.15, bf16[1,3,2816]{2,1,0:T(4,128)(2,1)S(1)} %copy.108, bf16[1,256,2816]{2,1,0:T(8,128)(2,1)} %bitcast.156, f32[2816]{0:T(1024)S(1)} %get-tuple-element.357, f32[256]{0:T(256)S(1)} %bitcast.177, f32[2816]{0:T(1024)S(1)} %get-tuple-element.358, ...), kind=kLoop, calls=%fused_computation.33 | loop fusion | flops 20905984 | bytes 4401664 | tf_op jit(solution)/shard_map/convert_element_type | solution.py:98
  66.1 2.6 fusion.17
  69.1 1.9 fusion.25
  72.3 1.4 copy.74
  73.7 146.0 %all-gather.4.cloned.1.call-done = f32[40960,128]{1,0:T(8,128)} async-done(((f32[2560,128]{1,0:T(8,128)}), f32[40960,128]{1,0:T(8,128)}) %all-gather.4.cloned.1.call-update) | async-done | bytes 20971536 | tf_op jit(solution)/shard_map/all_gather | solution.py:122
  219.8 38.9 %fusion.6 = f32[2560,1,128]{2,1,0:T(1,128)S(1)} fusion(f32[16,2560,1]{0,2,1:T(1,128)S(1)} %bitcast.154, f32[16,2560,128]{2,1,0:T(8,128)} %bitcast.150), kind=kOutput, calls=%fused_computation.15 | convolution fusion | flops 62914560 | bytes 22446080 | tf_op jit(solution)/shard_map/ick,ckn->ikn/dot_general | solution.py:119
  258.7 20.2 %while.17 = (s32[]{:T(128)}, bf16[3,2560,128]{2,1,0:T(8,128)(2,1)}, s32[3]{0:T(128)S(1)}, s32[3]{0:T(128)S(1)}, s32[1]{0:T(128)}, /*index=5*/bf16[1,256,2560]{1,...) while((s32[]{:T(128)}, bf16[3,2560,128]{2,1,0:T(8,128)(2,1)}, ...), condition=%wide.region_13.14_spmd, body=%wide.region_10.13_spmd.sunk | while | flops 170742112 | bytes 7442075 | solution.py:194
  263.1 4.0 %conditional.2 = (bf16[1,2560,128]{2,1,0:T(8,128)(2,1)S(1)}) conditional(s32[]{:T(128)} %bitcast.146, () %tuple.66, (bf16[1,256,2560]{1,2,0:T(8,128)(2,1)}, s32[]{:T(128)}, s32[1,256]{1,0:T(1,128)S(1)}, s32[]{:T(128)}, s32[]{:T(128)}, /*index=5*/f32[1,256,40]{1,2,0:T(8,128)S(1)}, bf16[1,256,128]{2,1,0:T(8,128)(2,1)S(1)}, s32[1]{0:T(128)}, ...), branch_computations={%region_11.11_spmd, %region_12.12_spmd} | conditional | flops 170742096 | bytes 6130356 | solution.py:192
  264.1 1.7 fusion.1
  279.0 1.7 broadcast_in_dim.192
  280.7 3.2 copy.79
  284.2 1.1 fusion.36
  285.3 5.1 %fusion.8 = f32[40,64,256]{2,1,0:T(8,128)} fusion(bf16[256,40,64]{0,2,1:T(8,128)(2,1)} %bitcast.30, f32[40,256]{1,0:T(8,128)S(1)} %bitcast.157, f32[256,256]{1,0:T(8,128)S(1)} %fusion.36, pred[256,256]{1,0:T(8,128)(4,1)S(1)} %fusion.34), kind=kOutput, calls=%fused_computation.18 | convolution fusion | flops 346030080 | bytes 4300800 | tf_op jit(solution)/shard_map/while/body/eval_jaxpr/hts,shp->thp/dot_general | solution.py:136
  290.3 3.4 copy.80
  293.7 4.6 %multiply_reduce_fusion = (f32[256]{0:T(256)S(1)}, f32[256,2560]{1,0:T(8,128)S(1)}) fusion(bf16[256,2560]{1,0:T(8,128)(2,1)S(1)} %copy-done.7, f32[2560]{0:T(1024)S(1)} %mul.239, bf16[1,256,2816]{2,1,0:T(8,128)(2,1)} %copy-done.1, f32[256,2560]{1,0:T(8,128)} %copy.80, f32[256,2560]{1,0:T(8,128)} %copy.79, f32[2560,128]{1,0:T(8,128)S(1)} %bitcast.149), kind=kOutput, calls=%fused_computation.40 | convolution fusion | flops 176619264 | bytes 11873280 | tf_op jit(solution)/shard_map/while/body/eval_jaxpr/dot_general | solution.py:142
  298.3 1.3 multiply_convert_fusion.3
  299.7 69.0 %reduce-scatter.2.cloned.1.call-done = bf16[160,3,128]{2,0,1:T(8,128)(2,1)} async-done(((bf16[2560,3,128]{2,0,1:T(8,128)(2,1)}), bf16[160,3,128]{2,0,1:T(8,128)(2,1)}) %reduce-scatter.2.cloned.1.call-update) | async-done | bytes 122896 | tf_op jit(solution)/shard_map/reduce_scatter | solution.py:195
  368.7 1.6 convert_bitcast_fusion.2
  (91 shorter events, 21.1 us)
Async XLA Ops:
  7.2 43.2 %copy-start.5 = (f32[40]{0:T(128)S(1)}, f32[40]{0:T(128)}, u32[]{:S(2)}) copy-start(f32[40]{0:T(128)} %param.22) | copy-start | bytes 484
  7.2 43.8 %copy-start.4 = (s32[16]{0:T(128)S(1)}, s32[16]{0:T(128)}, u32[]{:S(2)}) copy-start(s32[16]{0:T(128)} %param.19) | copy-start | bytes 196
  8.8 51.1 %all-to-all-start = ((bf16[16,1,3,2816]{3,2,1,0:T(4,128)(2,1)}), bf16[16,1,3,2816]{3,2,1,0:T(4,128)(2,1)S(1)}, u32[]{:S(2)}, u32[]{:S(2)}) async-start(bf16[16,1,3,2816]{3,2,1,0:T(4,128)(2,1)} %stack.2), calls=%async_computation | async-start | bytes 720896 | tf_op jit(solution)/shard_map/all_to_all | solution.py:20
  18.1 201.7 %all-gather.4.cloned.1.call-start = ((), (), s32[]{:S(2)}) async-start(), calls=%async_computation.3 | async-start | bytes 22282240 | tf_op jit(solution)/shard_map/all_gather | solution.py:122
  57.7 2.4 copy-start.3
  66.1 153.7 %copy-start.1 = (bf16[1,256,2816]{2,1,0:T(8,128)(2,1)}, bf16[1,256,2816]{2,1,0:T(8,128)(2,1)S(1)}, u32[]{:S(2)}) copy-start(bf16[1,256,2816]{2,1,0:T(8,128)(2,1)S(1)} %multiply_convert_fusion.2) | copy-start | bytes 4325380
  66.1 3.0 copy-start
  71.0 297.7 %reduce-scatter.2.cloned.1.call-start = ((), (), s32[]{:S(2)}) async-start(), calls=%async_computation.2 | async-start | bytes 2088960 | tf_op jit(solution)/shard_map/reduce_scatter | solution.py:195
  280.7 3.2 copy-start.6
  290.3 3.4 copy-start.7
  293.7 4.6 %copy-start.2 = (f32[2560]{0:T(1024)S(1)}, f32[2560]{0:T(1024)}, u32[]{:S(2)}) copy-start(f32[2560]{0:T(1024)} %param.25) | copy-start | bytes 30724
Sparse Core Ops, SparseCore 0:
  71.1 148.5 all-gather.3
  279.0 89.6 reduce-scatter.1
